TPU v7x, 512 devices: a whole 4x8x8 slice. The times are simulated.
512 devices in a mesh: worker: 16 (over x, z_lo, core), fsdp: 32 (over z_hi, y).
Axes of the slice: x: 4, y: 8, z: 8 (z_hi: 4, z_lo: 2; z = z_hi * 2 + z_lo), core: 2. Of those that a mesh axis runs over, the one named last changes fastest.
Arguments:
- hidden: bfloat16 [9472, 65536], P('fsdp', 'worker'), may hold values from -6 to 6
- cotangent: bfloat16 [65536, 1792], P(('worker', 'fsdp')), may hold values from -6 to 6
- first_moment: bfloat16 [16, 9472, 1792], P('worker', 'fsdp'), may hold values from -0.0625 to 0.0625
- second_moment: bfloat16 [16, 9472, 1792], P('worker', 'fsdp'), may hold values from 1.21593475e-05 to 0.00024414062
- outer_momentum: bfloat16 [9472, 1792], P('fsdp', 'worker'), may hold values from -4 to 4
Outputs:
- new_momentum: float32 [9472, 1792], P('fsdp', 'worker')
All inputs are finite; a program needn't handle non-finite values.
Results may differ from a plain program's by a relative error of at most 0.0003.
Values may be sent and summed in bfloat16 or wider, within the bound.
No kernel may reach another device: no remote copies, remote signals or barrier semaphores. Data moves between devices by JAX's collectives and lax.ppermute only.
A program may use at most 64 MiB of HBM per device.

v0:
```python
import jax
import jax.numpy as jnp
from jax import lax
from jax.sharding import Mesh
from jax.sharding import PartitionSpec as P

W = ("wx", "wz", "wc")
F = ("fz", "fy")
SPLIT = {"worker": (4, 2, 2), "fsdp": (4, 8)}


def shards(hidden, cotangent, first_moment, second_moment, outer_momentum):
    gathered = lax.all_gather(cotangent, ("fy", "fz"), axis=0, tiled=True)
    nz, ny = SPLIT["fsdp"]
    rows, tokens = hidden.shape
    reordered = (
        hidden.reshape(rows, nz, ny, tokens // (nz * ny))
        .transpose(0, 2, 1, 3)
        .reshape(rows, tokens)
    )
    gradient = jnp.dot(reordered, gathered, preferred_element_type=jnp.float32) / gathered.shape[0]
    first_new = 0.9 * first_moment[0].astype(jnp.float32) + 0.1 * gradient
    second_new = 0.95 * second_moment[0].astype(jnp.float32) + 0.05 * gradient * gradient
    pseudo = first_new / (jnp.sqrt(second_new) + 1e-08)
    workers = lax.axis_size(W)
    cols = pseudo.shape[1]
    blocks = pseudo.reshape(rows, workers, cols // workers)
    received = lax.all_to_all(blocks, W, 1, 1, tiled=True)
    average = received.sum(axis=1) / workers
    return 0.9 * outer_momentum.astype(jnp.float32) + average


def solution(mesh):
    fine = Mesh(mesh.devices.reshape(SPLIT["worker"] + SPLIT["fsdp"]), W + F)
    in_specs = (P(F, W), P(W + F, None), P(W, F, None), P(W, F, None), P(F, W))
    out_specs = P(F, W)
    return jax.shard_map(shards, mesh=fine, in_specs=in_specs, out_specs=out_specs, check_vma=False)
```

profile of v0, /device:TPU:1, one launch (start us, length us, event | category | flops | bytes accessed | tf_op | source)
XLA Modules:
  0.0 275.4 jit_solution(3912588997436417546)
XLA Ops:
  6.5 0.0 all-gather.2.cloned.1.call-start
  6.5 0.7 all-gather.2.cloned.1.call-update
  7.3 2.2 copy.9
  9.5 1.2 copy.11
  10.7 0.0 copy-start.1
  10.7 3.2 %reshape.16 = bf16[296,4096]{1,0:T(8,128)(2,1)} reshape(bf16[296,8,4,128]{3,2,1,0:T(4,128)(2,1)S(1)} %bitcast.20) | data formatting | bytes 4849664 | tf_op jit(solution)/shard_map/reshape | solution.py:19
  14.0 177.4 %all-gather.2.cloned.1.call-done = bf16[4096,1792]{1,0:T(8,128)(2,1)} async-done(((bf16[128,1792]{1,0:T(8,128)(2,1)}), bf16[4096,1792]{1,0:T(8,128)(2,1)}) %all-gather.2.cloned.1.call-update) | async-done | bytes 14680080 | tf_op jit(solution)/shard_map/all_gather | solution.py:13
  191.3 0.0 copy-done.1
  191.3 12.9 %fusion.2 = f32[296,1792]{1,0:T(8,128)} fusion(bf16[1,296,1792]{2,1,0:T(8,128)(2,1)S(1)} %copy-done.1, bf16[1,296,1792]{2,1,0:T(8,128)(2,1)} %param.7, bf16[296,4096]{1,0:T(8,128)(2,1)} %reshape.16, bf16[4096,1792]{1,0:T(8,128)(2,1)} %all-gather.2.cloned.1.call-done), kind=kOutput, calls=%fused_computation.4 | convolution fusion | flops 4351664128 | bytes 21348352 | tf_op jit(solution)/shard_map/dot_general | solution.py:21
  204.2 3.0 %reshape.17 = f32[296,16,112]{2,1,0:T(8,128)S(1)} reshape(f32[296,1792]{1,0:T(8,128)} %fusion.2) | data formatting | bytes 4243456 | tf_op jit(solution)/shard_map/reshape | solution.py:27
  207.2 0.8 copy.8
  208.0 59.0 %all_to_all.5 = f32[296,16,112]{2,0,1:T(8,128)S(1)} all-to-all(f32[296,16,112]{2,0,1:T(8,128)S(1)} %copy.8), channel_id=1, replica_groups=mesh['wx'=4,'wz'=2,'wc'=2,'fz'=4,'fy'=8] {'wx','wz','wc'}, dimensions={1} | all-to-all | bytes 4243456 | tf_op jit(solution)/shard_map/all_to_all | solution.py:28
  267.0 0.0 copy-start
  267.0 0.2 reduce_sum.9
  267.2 0.7 copy-done
  267.9 0.7 multiply_add_fusion
Async XLA Ops:
  6.5 184.8 %all-gather.2.cloned.1.call-start = ((), (), s32[]{:S(2)}) async-start(), calls=%async_computation.1 | async-start | bytes 15138816 | tf_op jit(solution)/shard_map/all_gather | solution.py:13
  10.7 180.6 %copy-start.1 = (bf16[1,296,1792]{2,1,0:T(8,128)(2,1)S(1)}, bf16[1,296,1792]{2,1,0:T(8,128)(2,1)}, u32[]{:S(2)}) copy-start(bf16[1,296,1792]{2,1,0:T(8,128)(2,1)} %param.8) | copy-start | bytes 3182596
  267.0 0.9 copy-start
Sparse Core Ops, SparseCore 0:
  10.5 180.7 all-gather.1
where the time goes:
time: 276 us; the launch traced here: 275 us
  waiting for transfers between devices  178 us (64%)
  blocking collectives  59 us (21%)
  between operations  13.4 us (5%)
  matrix products  12.9 us (5%)
  local copies, waits for them, and re-layouts  11.2 us (4%)
    all_gather x1, waiting for transfers between devices, shards(): gathered = lax.all_gather(cotangent, ('fy', 'fz'), axis=0, tiled=True)  177 us
    all_to_all x1, blocking collectives, shards(): received = lax.all_to_all(blocks, W, 1, 1, tiled=True)  59 us
    dot_general x1, matrix products, shards(): jnp.dot(reordered, gathered, preferred_element_type=jnp.float32)  12.9 us
  transfers between devices with their start and end apart: 1, of which 1 were waited for; matrix products, arithmetic and copies ran while one was open for 2% of the time, Pallas kernels for 0%

commit v1 on v0

--- a/solution.py
+++ b/solution.py
@@ -7,6 +7,9 @@
 W = ("wx", "wz", "wc")
 F = ("fz", "fy")
 SPLIT = {"worker": (4, 2, 2), "fsdp": (4, 8)}
+supply_the_ranges = lambda panel: jnp.concatenate(
+    lax.all_to_all(jnp.stack(jnp.split(panel, lax.axis_size(W), axis=1)), W, 0, 0), axis=1
+)
 
 
 def shards(hidden, cotangent, first_moment, second_moment, outer_momentum):
@@ -25,7 +28,7 @@
     workers = lax.axis_size(W)
     cols = pseudo.shape[1]
     blocks = pseudo.reshape(rows, workers, cols // workers)
-    received = lax.all_to_all(blocks, W, 1, 1, tiled=True)
+    received = supply_the_ranges(blocks)
     average = received.sum(axis=1) / workers
     return 0.9 * outer_momentum.astype(jnp.float32) + average
 

time: 276 us -> 277 us (level)
  no operation moved by 1% of the time
where the time goes in v1:
time: 277 us
  waiting for transfers between devices  178 us (64%)
  blocking collectives  59 us (21%)
  between operations  13.6 us (5%)
  matrix products  12.9 us (5%)
  local copies, waits for them, and re-layouts  12.3 us (4%)
    all_gather x1, waiting for transfers between devices, shards(): gathered = lax.all_gather(cotangent, ('fy', 'fz'), axis=0, tiled=True)  177 us
    all_to_all x1, blocking collectives, lax.all_to_all(jnp.stack(jnp.split(panel, lax.axis_size(W), axis=1)), W,...  59 us
    dot_general x1, matrix products, shards(): jnp.dot(reordered, gathered, preferred_element_type=jnp.float32)  12.9 us
  transfers between devices with their start and end apart: 1, of which 1 were waited for; matrix products, arithmetic and copies ran while one was open for 2% of the time, Pallas kernels for 0%

profile of v1, /device:TPU:1, one launch (start us, length us, event | category | flops | bytes accessed | tf_op | source)
XLA Modules:
  0.0 276.7 jit_solution(4616423825716961269)
XLA Ops:
  6.5 0.0 all-gather.2.cloned.1.call-start
  6.5 0.7 all-gather.2.cloned.1.call-update
  7.3 2.2 copy.52
  9.5 1.2 copy.54
  10.7 0.0 copy-start.1
  10.7 3.2 %reshape.18 = bf16[296,4096]{1,0:T(8,128)(2,1)} reshape(bf16[296,8,4,128]{3,2,1,0:T(4,128)(2,1)S(1)} %bitcast.66) | data formatting | bytes 4849664 | tf_op jit(solution)/shard_map/reshape | solution.py:22
  14.0 177.3 %all-gather.2.cloned.1.call-done = bf16[4096,1792]{1,0:T(8,128)(2,1)} async-done(((bf16[128,1792]{1,0:T(8,128)(2,1)}), bf16[4096,1792]{1,0:T(8,128)(2,1)}) %all-gather.2.cloned.1.call-update) | async-done | bytes 14680080 | tf_op jit(solution)/shard_map/all_gather | solution.py:16
  191.3 0.0 copy-done.1
  191.3 12.9 %fusion.2 = f32[296,1792]{1,0:T(8,128)} fusion(bf16[1,296,1792]{2,1,0:T(8,128)(2,1)S(1)} %copy-done.1, bf16[1,296,1792]{2,1,0:T(8,128)(2,1)} %param.7, bf16[296,4096]{1,0:T(8,128)(2,1)} %reshape.18, bf16[4096,1792]{1,0:T(8,128)(2,1)} %all-gather.2.cloned.1.call-done), kind=kOutput, calls=%fused_computation.4 | convolution fusion | flops 4351664128 | bytes 21348352 | tf_op jit(solution)/shard_map/dot_general | solution.py:24
  204.2 3.0 %reshape.19 = f32[296,16,112]{2,1,0:T(8,128)S(1)} reshape(f32[296,1792]{1,0:T(8,128)} %fusion.2) | data formatting | bytes 4243456 | tf_op jit(solution)/shard_map/reshape | solution.py:30
  207.2 1.7 fusion.3
  209.3 59.0 %all_to_all.5 = f32[16,296,1,112]{3,1,2,0:T(8,128)S(1)} all-to-all(f32[16,296,1,112]{3,1,2,0:T(8,128)S(1)} %constant_dynamic-update-slice_fusion), channel_id=1, replica_groups=mesh['wx'=4,'wz'=2,'wc'=2,'fz'=4,'fy'=8] {'wx','wz','wc'}, dimensions={0} | all-to-all | bytes 4243456 | tf_op jit(solution)/shard_map/all_to_all | solution.py:11
  268.3 0.0 copy-start
  268.3 0.2 reduce_sum.9
  268.4 0.7 copy-done
  269.1 0.7 multiply_add_fusion
  (16 shorter events, 0.2 us)
Async XLA Ops:
  6.5 184.8 %all-gather.2.cloned.1.call-start = ((), (), s32[]{:S(2)}) async-start(), calls=%async_computation.1 | async-start | bytes 15138816 | tf_op jit(solution)/shard_map/all_gather | solution.py:16
  10.7 180.6 %copy-start.1 = (bf16[1,296,1792]{2,1,0:T(8,128)(2,1)S(1)}, bf16[1,296,1792]{2,1,0:T(8,128)(2,1)}, u32[]{:S(2)}) copy-start(bf16[1,296,1792]{2,1,0:T(8,128)(2,1)} %param.8) | copy-start | bytes 3182596
  268.3 0.9 copy-start
Sparse Core Ops, SparseCore 0:
  10.5 180.7 all-gather.1
